TPU v7x, 512 devices: a whole 4x8x8 slice. The times are simulated.
512 devices in a mesh: wide: 32 (over z, x), narrow: 16 (over y, core).
Axes of the slice: x: 4, y: 8, z: 8, core: 2. Of those that a mesh axis runs over, the one named last changes fastest.
Arguments:
- tokens: bfloat16 [1024, 16384], P('wide', 'narrow'), may hold values from -200 to 200
- norm_gain: float32 [16384], P('narrow'), may hold values from 0.25 to 1.75
- gate_weight: bfloat16 [26624, 16384], P('wide', 'narrow'), may hold values from -0.046875 to 0.046875
- up_weight: bfloat16 [26624, 16384], P('wide', 'narrow'), may hold values from -0.046875 to 0.046875
- down_weight: bfloat16 [26624, 16384], P('wide', 'narrow'), may hold values from -0.0390625 to 0.0390625
Outputs:
- ffn_out: bfloat16 [1024, 16384], P('wide', 'narrow')
All inputs are finite; a program needn't handle non-finite values.
Results may differ from a plain program's by a relative error of at most 0.03.
Values may be sent and summed in bfloat16 or wider, within the bound.
No kernel may reach another device: no remote copies, remote signals or barrier semaphores. Data moves between devices by JAX's collectives and lax.ppermute only.
A program may use at most 64 MiB of HBM per device.

v0:
```python
import jax
import jax.numpy as jnp
from jax import lax
from jax.sharding import PartitionSpec as P

D = 16384


EPS = 1e-05


def project_pair(rows, gate_weight, up_weight):
    dims = (((1,), (1,)), ((), ()))
    gate = lax.dot_general(rows, gate_weight, dims, preferred_element_type=jnp.float32)
    upward = lax.dot_general(rows, up_weight, dims, preferred_element_type=jnp.float32)
    return jnp.concatenate([gate, upward], axis=1)


def activate(sums, width):
    return (jax.nn.silu(sums[:, :width]) * sums[:, width:]).astype(jnp.bfloat16)


def local(tokens, norm_gain, gate_weight, up_weight, down_weight):
    width = gate_weight.shape[0]
    whole = lax.all_gather(tokens, "wide", axis=0, tiled=True)
    values = whole.astype(jnp.float32)
    squares = lax.psum(jnp.sum(values * values, axis=1), "narrow")
    normed = (values * lax.rsqrt(squares[:, None] / D + EPS) * norm_gain).astype(jnp.bfloat16)
    sums = lax.psum(
        project_pair(normed, gate_weight, up_weight).astype(jnp.bfloat16), "narrow"
    ).astype(jnp.float32)
    hidden = activate(sums, width)
    return lax.psum_scatter(
        jnp.dot(hidden, down_weight, preferred_element_type=jnp.float32).astype(jnp.bfloat16),
        "wide",
        scatter_dimension=0,
        tiled=True,
    )


def solution(mesh):
    in_specs = (
        P("wide", "narrow"),
        P("narrow"),
        P("wide", "narrow"),
        P("wide", "narrow"),
        P("wide", "narrow"),
    )
    out_specs = P("wide", "narrow")
    return jax.shard_map(local, mesh=mesh, in_specs=in_specs, out_specs=out_specs, check_vma=False)
```

profile of v0, /device:TPU:16, one launch (start us, length us, event | category | flops | bytes accessed | tf_op | source)
XLA Modules:
  0.0 490.7 jit_solution(1981325503855157326)
XLA Ops:
  6.5 0.0 copy-start
  6.5 0.0 all-gather.2.cloned.1.call-start
  6.5 0.7 all-gather.2.cloned.1.call-update
  7.3 0.0 all-reduce.2.cloned.1.call-start
  7.3 91.7 %all-gather.2.cloned.1.call-done = bf16[1024,1024]{1,0:T(8,128)(2,1)} async-done(((bf16[32,1024]{1,0:T(8,128)(2,1)}), bf16[1024,1024]{1,0:T(8,128)(2,1)}) %all-gather.2.cloned.1.call-update) | async-done | bytes 2097168 | tf_op jit(solution)/shard_map/all_gather | solution.py:25
  99.0 2.1 fusion
  101.1 20.3 %psum.14 = f32[1024]{0:T(1024)S(1)} all-reduce(f32[1024]{0:T(1024)S(1)} %fusion), channel_id=1, replica_groups=mesh['wide'=32,'narrow'=16] {'narrow'}, use_global_device_ids=true, to_apply=%region_1.0 | all-reduce | flops 1024 | bytes 8192 | tf_op jit(solution)/shard_map/psum | solution.py:27
  121.4 0.0 copy-start.1
  121.4 0.0 copy-start.2
  121.5 0.0 copy-start.3
  121.5 4.3 convolution_convert_fusion.1
  125.8 0.0 copy-done.1
  125.8 0.0 copy-done.2
  125.8 0.0 copy-done.3
  125.8 2.1 convolution_convert_fusion.2
  127.9 2.1 pad_maximum_fusion
  130.0 0.0 all-reduce.2.cloned.1.call-update
  130.0 0.0 reduce-scatter.2.cloned.1.call-start
  130.1 122.1 %all-reduce.2.cloned.1.call-done = bf16[1024,1664]{0,1:T(8,128)(2,1)} async-done(((bf16[1024,1664]{0,1:T(8,128)(2,1)}), bf16[1024,1664]{0,1:T(8,128)(2,1)}) %all-reduce.2.cloned.1.call-update) | async-done | bytes 3407888 | tf_op jit(solution)/shard_map/psum | solution.py:29
  252.2 2.8 convert_element_type.18
  255.0 0.0 copy-done
  255.0 3.9 convolution_convert_fusion
  258.9 0.0 reduce-scatter.2.cloned.1.call-update
  258.9 225.3 %reduce-scatter.2.cloned.1.call-done = bf16[32,1024]{1,0:T(8,128)(2,1)} async-done(((bf16[1024,1024]{1,0:T(8,128)(2,1)}), bf16[32,1024]{1,0:T(8,128)(2,1)}) %reduce-scatter.2.cloned.1.call-update) | async-done | bytes 65552 | tf_op jit(solution)/shard_map/reduce_scatter | solution.py:33
  (1 shorter events, 0.0 us)
Async XLA Ops:
  6.5 248.4 %copy-start = (bf16[832,1024]{1,0:T(8,128)(2,1)S(1)}, bf16[832,1024]{1,0:T(8,128)(2,1)}, u32[]{:S(2)}) copy-start(bf16[832,1024]{1,0:T(8,128)(2,1)} %param.9) | copy-start | bytes 5111812
  6.5 92.5 %all-gather.2.cloned.1.call-start = ((), (), s32[]{:S(2)}) async-start(), calls=%async_computation.1 | async-start | bytes 2162688 | tf_op jit(solution)/shard_map/all_gather | solution.py:25
  7.3 245.0 %all-reduce.2.cloned.1.call-start = ((), (), s32[]{:S(2)}) async-start(), calls=%async_computation.2 | async-start | bytes 6815744 | tf_op jit(solution)/shard_map/psum | solution.py:29
  121.4 4.3 copy-start.1
  121.4 4.3 copy-start.2
  121.5 4.3 copy-start.3
  130.0 354.1 %reduce-scatter.2.cloned.1.call-start = ((), (), s32[]{:S(2)}) async-start(), calls=%async_computation.3 | async-start | bytes 2162688 | tf_op jit(solution)/shard_map/reduce_scatter | solution.py:33
Sparse Core Ops, SparseCore 0:
  10.5 88.4 all-gather.1
  130.2 122.0 all-reduce.1
  259.0 225.0 reduce-scatter.1
where the time goes:
time: 491 us
  waiting for transfers between devices  440 us (90%)
  blocking collectives  20.3 us (4%)
  between operations  13.2 us (3%)
  matrix products  10.3 us (2%)
  other arithmetic  6.94 us (1%)
    reduce_scatter x1, waiting for transfers between devices, local(): lax.psum_scatter(jnp.dot(hidden, down_weight, preferred_element_type=jnp....  225 us
    psum x1, waiting for transfers between devices, local(): lax.psum(project_pair(normed, gate_weight, up_weight).astype(jnp.bfloat16...  122 us
    all_gather x1, waiting for transfers between devices, local(): whole = lax.all_gather(tokens, 'wide', axis=0, tiled=True)  91.7 us
    psum x1, blocking collectives, local(): squares = lax.psum(jnp.sum(values * values, axis=1), 'narrow')  20.3 us
  transfers between devices with their start and end apart: 3, of which 3 were waited for; matrix products, arithmetic and copies ran while one was open for 0% of the time, Pallas kernels for 0%

commit v1 on v0

v1 whole, which is shorter than its diff:
```python
import jax
import jax.numpy as jnp
from jax import lax
from jax.sharding import PartitionSpec as P

D = 16384
EPS = 1e-05

WIDE_AG = 'a2a'
NARROW = 'rs_ag'
WIDE_RS = 'a2a'


def local(tokens, norm_gain, gate_weight, up_weight, down_weight):
    width = gate_weight.shape[0]
    n_wide = lax.axis_size("wide")
    n_narrow = lax.axis_size("narrow")
    rows = tokens.shape[0]
    if WIDE_AG == "a2a":
        spread = jnp.broadcast_to(tokens[None], (n_wide,) + tokens.shape)
        whole = lax.all_to_all(spread, "wide", 0, 0).reshape(n_wide * rows, tokens.shape[1])
    else:
        whole = lax.all_gather(tokens, "wide", axis=0, tiled=True)
    values = whole.astype(jnp.float32)
    squares = lax.psum(jnp.sum(values * values, axis=1), "narrow")
    normed = (values * lax.rsqrt(squares[:, None] / D + EPS) * norm_gain).astype(jnp.bfloat16)
    dims = (((1,), (1,)), ((), ()))
    gate = lax.dot_general(normed, gate_weight, dims, preferred_element_type=jnp.float32)
    upward = lax.dot_general(normed, up_weight, dims, preferred_element_type=jnp.float32)
    pair = jnp.concatenate([gate, upward], axis=1).astype(jnp.bfloat16)
    total = whole.shape[0]
    if NARROW == "ar":
        sums = lax.psum(pair, "narrow").astype(jnp.float32)
        hidden = (jax.nn.silu(sums[:, :width]) * sums[:, width:]).astype(jnp.bfloat16)
    else:
        if NARROW == "rs_ag":
            part = lax.psum_scatter(pair, "narrow", scatter_dimension=0, tiled=True).astype(jnp.float32)
        else:
            pieces = pair.reshape(n_narrow, total // n_narrow, 2 * width)
            part = jnp.sum(lax.all_to_all(pieces, "narrow", 0, 0).astype(jnp.float32), axis=0)
        mine = (jax.nn.silu(part[:, :width]) * part[:, width:]).astype(jnp.bfloat16)
        hidden = lax.all_gather(mine, "narrow", axis=0, tiled=True)
    down = jnp.dot(hidden, down_weight, preferred_element_type=jnp.float32).astype(jnp.bfloat16)
    if WIDE_RS == "a2a":
        pieces = down.reshape(n_wide, total // n_wide, down.shape[1])
        return jnp.sum(lax.all_to_all(pieces, "wide", 0, 0).astype(jnp.float32), axis=0).astype(jnp.bfloat16)
    return lax.psum_scatter(down, "wide", scatter_dimension=0, tiled=True)


def solution(mesh):
    in_specs = (
        P("wide", "narrow"),
        P("narrow"),
        P("wide", "narrow"),
        P("wide", "narrow"),
        P("wide", "narrow"),
    )
    out_specs = P("wide", "narrow")
    return jax.shard_map(local, mesh=mesh, in_specs=in_specs, out_specs=out_specs, check_vma=False)
```

time: 491 us -> 290 us (0.59)
  the two profiles are of different devices: /device:TPU:16 before, /device:TPU:2 now
where the time goes in v1:
time: 290 us; the launch traced here: 289 us
  blocking collectives  150 us (52%)
  waiting for transfers between devices  101 us (35%)
  between operations  13.5 us (5%)
  other arithmetic  9.17 us (3%)
  local copies, waits for them, and re-layouts  8.24 us (3%)
  matrix products  7.85 us (3%)
    all_to_all x1, blocking collectives, local(): lax.all_to_all(spread, 'wide', 0, 0).reshape(n_wide * rows, tokens.shape[1])  63.8 us
    all_to_all x1, blocking collectives, local(): lax.all_to_all(pieces, 'wide', 0, 0).astype(jnp.float32)  61.4 us
    reduce_scatter x1, waiting for transfers between devices, local(): lax.psum_scatter(pair, 'narrow', scatter_dimension=0, tiled=True)  59.5 us
    all_gather x1, waiting for transfers between devices, local(): hidden = lax.all_gather(mine, 'narrow', axis=0, tiled=True)  41.3 us
    psum x1, blocking collectives, local(): squares = lax.psum(jnp.sum(values * values, axis=1), 'narrow')  24.5 us
    unnamed x11, local copies, waits for them, and re-layouts  6.95 us
  transfers between devices with their start and end apart: 2, of which 2 were waited for; matrix products, arithmetic and copies ran while one was open for 0% of the time, Pallas kernels for 0%

profile of v1, /device:TPU:2, one launch (start us, length us, event | category | flops | bytes accessed | tf_op | source)
XLA Modules:
  0.0 289.3 jit_solution(1140043333957172193)
XLA Ops:
  6.5 0.0 copy-start
  6.5 0.0 reduce-scatter.4.cloned.1.call-start
  6.5 1.2 broadcast_in_dim.2
  7.8 63.8 %all_to_all.10 = bf16[32,32,1024]{2,1,0:T(8,128)(2,1)S(1)} all-to-all(bf16[32,32,1024]{2,1,0:T(8,128)(2,1)S(1)} %broadcast_in_dim.2), channel_id=1, replica_groups=mesh['wide'=32,'narrow'=16] {'wide'}, dimensions={0} | all-to-all | bytes 4194304 | tf_op jit(solution)/shard_map/all_to_all | solution.py:21
  71.6 0.0 copy-start.1
  71.6 1.3 copy-done.1
  72.9 0.0 copy-start.2
  72.9 0.5 multiply_reduce_fusion
  73.4 0.1 reduce_sum.24
  73.5 24.5 %psum.7 = f32[1024]{0:T(1024)S(1)} all-reduce(f32[1024]{0:T(1024)S(1)} %reduce_sum.24), channel_id=1, replica_groups=mesh['wide'=32,'narrow'=16] {'narrow'}, use_global_device_ids=true, to_apply=%region_1.0 | all-reduce | flops 1024 | bytes 8192 | tf_op jit(solution)/shard_map/psum | solution.py:25
  97.9 0.0 copy-done.2
  97.9 0.0 copy-start.3
  98.0 2.3 fusion.1
  100.2 0.0 copy-done.3
  100.2 0.0 copy-start.4
  100.2 2.0 convolution_convert_fusion.1
  102.3 0.0 copy-done.4
  102.3 2.0 convolution_convert_fusion.2
  104.3 2.1 pad_maximum_fusion
  106.4 5.6 %copy.9 = bf16[1024,1664]{1,0:T(8,128)(2,1)} copy(bf16[1024,1664]{0,1:T(8,128)(2,1)} %pad_maximum_fusion) | data formatting | bytes 6815744
  112.0 0.0 reduce-scatter.4.cloned.1.call-update
  112.0 0.0 all-gather.2.cloned.1.call-start
  112.0 59.5 %reduce-scatter.4.cloned.1.call-done = bf16[64,1664]{1,0:T(8,128)(2,1)} async-done(((bf16[1024,1664]{1,0:T(8,128)(2,1)}), bf16[64,1664]{1,0:T(8,128)(2,1)}) %reduce-scatter.4.cloned.1.call-update) | async-done | bytes 213008 | tf_op jit(solution)/shard_map/reduce_scatter | solution.py:37
  171.6 1.0 convert_element_type.28
  172.5 0.8 fusion.2
  173.3 0.0 all-gather.2.cloned.1.call-update
  173.3 41.3 %all-gather.2.cloned.1.call-done = bf16[1024,832]{1,0:T(8,128)(2,1)} async-done(((bf16[64,832]{1,0:T(8,128)(2,1)}), bf16[1024,832]{1,0:T(8,128)(2,1)}) %all-gather.2.cloned.1.call-update) | async-done | bytes 1703952 | tf_op jit(solution)/shard_map/all_gather | solution.py:42
  214.7 0.0 copy-done
  214.7 3.8 %convolution_convert_fusion = bf16[1024,1024]{1,0:T(8,128)(2,1)S(1)} fusion(bf16[1024,832]{1,0:T(8,128)(2,1)} %all-gather.2.cloned.1.call-done, bf16[832,1024]{1,0:T(8,128)(2,1)S(1)} %copy-done), kind=kOutput, calls=%fused_computation.5 | convolution fusion | flops 1745879040 | bytes 5505024 | tf_op jit(solution)/shard_map/dot_general | solution.py:43
  218.5 61.4 %all_to_all.11 = bf16[32,32,1024]{2,1,0:T(8,128)(2,1)} all-to-all(bf16[32,32,1024]{2,1,0:T(8,128)(2,1)S(1)} %bitcast.14), channel_id=1, replica_groups=mesh['wide'=32,'narrow'=16] {'wide'}, dimensions={0} | all-to-all | bytes 4194304 | tf_op jit(solution)/shard_map/all_to_all | solution.py:46
  279.9 2.6 reduce_sum.25
  (1 shorter events, 0.0 us)
Async XLA Ops:
  6.5 208.1 %copy-start = (bf16[832,1024]{1,0:T(8,128)(2,1)S(1)}, bf16[832,1024]{1,0:T(8,128)(2,1)}, u32[]{:S(2)}) copy-start(bf16[832,1024]{1,0:T(8,128)(2,1)} %param.9) | copy-start | bytes 5111812
  6.5 165.0 %reduce-scatter.4.cloned.1.call-start = ((), (), s32[]{:S(2)}) async-start(), calls=%async_computation.4 | async-start | bytes 3620864 | tf_op jit(solution)/shard_map/reduce_scatter | solution.py:37
  71.6 1.4 copy-start.1
  72.9 25.0 %copy-start.2 = (f32[1024]{0:T(1024)S(1)}, f32[1024]{0:T(1024)}, u32[]{:S(2)}) copy-start(f32[1024]{0:T(1024)} %param.6) | copy-start | bytes 12292
  97.9 2.3 copy-start.3
  100.2 2.0 copy-start.4
  112.0 102.7 %all-gather.2.cloned.1.call-start = ((), (), s32[]{:S(2)}) async-start(), calls=%async_computation.3 | async-start | bytes 1949696 | tf_op jit(solution)/shard_map/all_gather | solution.py:42
Sparse Core Ops, SparseCore 0:
  112.1 59.4 reduce-scatter.3
  173.9 40.7 all-gather.1

commit v2 on v0

v2 whole, which is shorter than its diff:
```python
import jax
import jax.numpy as jnp
from jax import lax
from jax.sharding import PartitionSpec as P

EPS = 1e-05


def local(tokens, norm_gain, gate_weight, up_weight, down_weight):
    width = gate_weight.shape[0]
    n_wide = lax.axis_size("wide")
    n_narrow = lax.axis_size("narrow")
    model_width = tokens.shape[1] * n_narrow
    rows = tokens.shape[0]
    spread = jnp.broadcast_to(tokens[None], (n_wide,) + tokens.shape)
    whole = lax.all_to_all(spread, "wide", 0, 0).reshape(n_wide * rows, tokens.shape[1])
    values = whole.astype(jnp.float32)
    partial = jnp.sum(values * values, axis=1)
    scaled = (values * norm_gain).astype(jnp.bfloat16)
    dims = (((1,), (1,)), ((), ()))
    gate = lax.dot_general(scaled, gate_weight, dims, preferred_element_type=jnp.float32)
    upward = lax.dot_general(scaled, up_weight, dims, preferred_element_type=jnp.float32)
    pair = jnp.concatenate([gate, upward], axis=1).astype(jnp.bfloat16)
    pair, partial = lax.optimization_barrier((pair, partial))
    part = lax.psum_scatter(pair, "narrow", scatter_dimension=0, tiled=True)
    squares = lax.psum(partial, "narrow")
    step = part.shape[0]
    start = lax.axis_index("narrow") * step
    mine_sq = lax.dynamic_slice_in_dim(squares, start, step, 0)
    scale = lax.rsqrt(mine_sq / model_width + EPS)[:, None]
    sums = part.astype(jnp.float32)
    mine = (jax.nn.silu(sums[:, :width] * scale) * (sums[:, width:] * scale)).astype(jnp.bfloat16)
    hidden = lax.all_gather(mine, "narrow", axis=0, tiled=True)
    down = jnp.dot(hidden, down_weight, preferred_element_type=jnp.float32).astype(jnp.bfloat16)
    pieces = down.reshape(n_wide, down.shape[0] // n_wide, down.shape[1])
    return jnp.sum(lax.all_to_all(pieces, "wide", 0, 0).astype(jnp.float32), axis=0).astype(jnp.bfloat16)


def solution(mesh):
    in_specs = (
        P("wide", "narrow"),
        P("narrow"),
        P("wide", "narrow"),
        P("wide", "narrow"),
        P("wide", "narrow"),
    )
    out_specs = P("wide", "narrow")
    return jax.shard_map(local, mesh=mesh, in_specs=in_specs, out_specs=out_specs, check_vma=False)
```

time: 491 us -> 266 us (0.54)
  the two profiles are of different devices: /device:TPU:16 before, /device:TPU:2 now
where the time goes in v2:
time: 266 us
  blocking collectives  150 us (56%)
  waiting for transfers between devices  77.5 us (29%)
  between operations  13.5 us (5%)
  other arithmetic  9.25 us (3%)
  local copies, waits for them, and re-layouts  8.37 us (3%)
  matrix products  7.76 us (3%)
    all_to_all x1, blocking collectives, local(): lax.all_to_all(spread, 'wide', 0, 0).reshape(n_wide * rows, tokens.shape[1])  63.8 us
    all_to_all x1, blocking collectives, local(): lax.all_to_all(pieces, 'wide', 0, 0).astype(jnp.float32)  61.4 us
    all_gather x1, waiting for transfers between devices, local(): hidden = lax.all_gather(mine, 'narrow', axis=0, tiled=True)  41.4 us
    reduce_scatter x1, waiting for transfers between devices, local(): part = lax.psum_scatter(pair, 'narrow', scatter_dimension=0, tiled=True)  36.1 us
    psum x1, blocking collectives, local(): squares = lax.psum(partial, 'narrow')  24.5 us
    unnamed x11, local copies, waits for them, and re-layouts  7.08 us
  transfers between devices with their start and end apart: 2, of which 2 were waited for; matrix products, arithmetic and copies ran while one was open for 0% of the time, Pallas kernels for 0%

profile of v2, /device:TPU:2, one launch (start us, length us, event | category | flops | bytes accessed | tf_op | source)
XLA Modules:
  0.0 266.1 jit_solution(2063783216898538441)
XLA Ops:
  6.5 0.0 copy-start
  6.5 0.0 reduce-scatter.4.cloned.1.call-start
  6.5 1.2 broadcast_in_dim.2
  7.8 63.8 %all_to_all.10 = bf16[32,32,1024]{2,1,0:T(8,128)(2,1)S(1)} all-to-all(bf16[32,32,1024]{2,1,0:T(8,128)(2,1)S(1)} %broadcast_in_dim.2), channel_id=1, replica_groups=mesh['wide'=32,'narrow'=16] {'wide'}, dimensions={0} | all-to-all | bytes 4194304 | tf_op jit(solution)/shard_map/all_to_all | solution.py:16
  71.6 0.0 copy-start.1
  71.6 1.3 copy-done.1
  72.9 0.0 copy-start.2
  72.9 0.5 multiply_reduce_fusion
  73.4 0.1 reduce_sum.24
  73.5 0.1 copy-done.2
  73.6 0.0 copy-start.3
  73.6 2.3 fusion
  75.9 0.0 copy-done.3
  75.9 0.0 copy-start.4
  75.9 2.0 convolution_convert_fusion.1
  77.9 0.0 copy-done.4
  77.9 2.0 convolution_convert_fusion.2
  79.8 2.1 pad_maximum_fusion
  81.9 5.6 %copy.9 = bf16[1024,1664]{1,0:T(8,128)(2,1)} copy(bf16[1024,1664]{0,1:T(8,128)(2,1)} %pad_maximum_fusion) | data formatting | bytes 6815744
  87.5 0.0 reduce-scatter.4.cloned.1.call-update
  87.5 0.0 all-gather.2.cloned.1.call-start
  87.6 24.5 %psum.7 = f32[1024]{0:T(1024)S(1)} all-reduce(f32[1024]{0:T(1024)S(1)} %reduce_sum.24), channel_id=1, replica_groups=mesh['wide'=32,'narrow'=16] {'narrow'}, use_global_device_ids=true, to_apply=%region_2.0 | all-reduce | flops 1024 | bytes 8192 | tf_op jit(solution)/shard_map/psum | solution.py:26
  112.1 0.1 add_rsqrt_fusion
  112.2 36.1 %reduce-scatter.4.cloned.1.call-done = bf16[64,1664]{1,0:T(8,128)(2,1)} async-done(((bf16[1024,1664]{1,0:T(8,128)(2,1)}), bf16[64,1664]{1,0:T(8,128)(2,1)}) %reduce-scatter.4.cloned.1.call-update) | async-done | bytes 213008 | tf_op jit(solution)/shard_map/reduce_scatter | solution.py:25
  148.2 1.0 convert_element_type.28
  149.2 0.8 fusion.2
  150.0 0.0 all-gather.2.cloned.1.call-update
  150.0 41.4 %all-gather.2.cloned.1.call-done = bf16[1024,832]{1,0:T(8,128)(2,1)} async-done(((bf16[64,832]{1,0:T(8,128)(2,1)}), bf16[1024,832]{1,0:T(8,128)(2,1)}) %all-gather.2.cloned.1.call-update) | async-done | bytes 1703952 | tf_op jit(solution)/shard_map/all_gather | solution.py:33
  191.4 0.0 copy-done
  191.4 3.8 %convolution_convert_fusion = bf16[1024,1024]{1,0:T(8,128)(2,1)S(1)} fusion(bf16[1024,832]{1,0:T(8,128)(2,1)} %all-gather.2.cloned.1.call-done, bf16[832,1024]{1,0:T(8,128)(2,1)S(1)} %copy-done), kind=kOutput, calls=%fused_computation.4 | convolution fusion | flops 1745879040 | bytes 5505024 | tf_op jit(solution)/shard_map/dot_general | solution.py:34
  195.3 61.4 %all_to_all.11 = bf16[32,32,1024]{2,1,0:T(8,128)(2,1)} all-to-all(bf16[32,32,1024]{2,1,0:T(8,128)(2,1)S(1)} %bitcast.12), channel_id=1, replica_groups=mesh['wide'=32,'narrow'=16] {'wide'}, dimensions={0} | all-to-all | bytes 4194304 | tf_op jit(solution)/shard_map/all_to_all | solution.py:36
  256.6 2.6 reduce_sum.25
Async XLA Ops:
  6.5 184.9 %copy-start = (bf16[832,1024]{1,0:T(8,128)(2,1)S(1)}, bf16[832,1024]{1,0:T(8,128)(2,1)}, u32[]{:S(2)}) copy-start(bf16[832,1024]{1,0:T(8,128)(2,1)} %param.9) | copy-start | bytes 5111812
  6.5 141.7 %reduce-scatter.4.cloned.1.call-start = ((), (), s32[]{:S(2)}) async-start(), calls=%async_computation.4 | async-start | bytes 3620864 | tf_op jit(solution)/shard_map/reduce_scatter | solution.py:25
  71.6 1.4 copy-start.1
  72.9 0.7 copy-start.2
  73.6 2.3 copy-start.3
  75.9 2.0 copy-start.4
  87.5 103.9 %all-gather.2.cloned.1.call-start = ((), (), s32[]{:S(2)}) async-start(), calls=%async_computation.3 | async-start | bytes 1949696 | tf_op jit(solution)/shard_map/all_gather | solution.py:33
Sparse Core Ops, SparseCore 0:
  87.7 60.5 reduce-scatter.3
  150.6 40.8 all-gather.1

commit v3 on v2

v3 whole, which is shorter than its diff:
```python
import jax
import jax.numpy as jnp
from jax import lax
from jax.sharding import Mesh, PartitionSpec as P

EPS = 1e-05
NARROW = ("y", "core")


def local(tokens, norm_gain, gate_weight, up_weight, down_weight):
    width = gate_weight.shape[0]
    n_z = lax.axis_size("z")
    n_x = lax.axis_size("x")
    n_narrow = lax.axis_size(NARROW)
    model_width = tokens.shape[1] * n_narrow
    rows = tokens.shape[0]
    spread = jnp.broadcast_to(tokens[None], (n_z,) + tokens.shape)
    near = lax.all_to_all(spread, "z", 0, 0)
    spread = jnp.broadcast_to(near[:, None], (n_z, n_x) + tokens.shape)
    whole = lax.all_to_all(spread, "x", 1, 1).reshape(n_z * n_x * rows, tokens.shape[1])
    values = whole.astype(jnp.float32)
    partial = jnp.sum(values * values, axis=1)
    scaled = (values * norm_gain).astype(jnp.bfloat16)
    dims = (((1,), (1,)), ((), ()))
    gate = lax.dot_general(scaled, gate_weight, dims, preferred_element_type=jnp.float32)
    upward = lax.dot_general(scaled, up_weight, dims, preferred_element_type=jnp.float32)
    pair = jnp.concatenate([gate, upward], axis=1).astype(jnp.bfloat16)
    pair, partial = lax.optimization_barrier((pair, partial))
    part = lax.psum_scatter(pair, NARROW, scatter_dimension=0, tiled=True)
    squares = lax.psum(partial, NARROW)
    step = part.shape[0]
    start = lax.axis_index(NARROW) * step
    mine_sq = lax.dynamic_slice_in_dim(squares, start, step, 0)
    scale = lax.rsqrt(mine_sq / model_width + EPS)[:, None]
    sums = part.astype(jnp.float32)
    mine = (jax.nn.silu(sums[:, :width] * scale) * (sums[:, width:] * scale)).astype(jnp.bfloat16)
    half = width // 2
    first = lax.all_gather(mine[:, :half], NARROW, axis=0, tiled=True)
    second = lax.all_gather(mine[:, half:], NARROW, axis=0, tiled=True)
    down = (jnp.dot(first, down_weight[:half], preferred_element_type=jnp.float32)
            + jnp.dot(second, down_weight[half:], preferred_element_type=jnp.float32)).astype(jnp.bfloat16)
    pieces = down.reshape(n_z, n_x, rows, down.shape[1])
    across = jnp.sum(lax.all_to_all(pieces, "x", 1, 1).astype(jnp.float32), axis=1).astype(jnp.bfloat16)
    return jnp.sum(lax.all_to_all(across, "z", 0, 0).astype(jnp.float32), axis=0).astype(jnp.bfloat16)


def solution(mesh):
    n_wide, n_narrow = mesh.devices.shape
    n_x = len({device.coords[0] for device in mesh.devices[:, 0]})
    view = Mesh(mesh.devices.reshape(n_wide // n_x, n_x, n_narrow // 2, 2), ("z", "x", "y", "core"))
    wide = ("z", "x")
    in_specs = (
        P(wide, NARROW),
        P(NARROW),
        P(wide, NARROW),
        P(wide, NARROW),
        P(wide, NARROW),
    )
    out_specs = P(wide, NARROW)
    return jax.shard_map(local, mesh=view, in_specs=in_specs, out_specs=out_specs, check_vma=False)
```

time: 266 us -> 246 us (0.925)
  waiting for transfers between devices: 77.5 us -> 36.5 us
  blocking collectives: 150 us -> 170 us
  local copies, waits for them, and re-layouts: 8.37 us -> 11.2 us
    all_gather x1 -> x0, waiting for transfers between devices: 41.4 us -> none  [local(): hidden = lax.all_gather(mine, 'narrow', axis=0, tiled=True)]
    all_gather x0 -> x2, blocking collectives: none -> 36.5 us  [the longest x1 18.7 us: local(): second = lax.all_gather(mine[:, half:], NARROW, axis=0, tiled=True)]
    unnamed x2, waiting for transfers between devices: 0.03 us -> 36.5 us
    reduce_scatter x1 -> x0, waiting for transfers between devices: 36.1 us -> none  [local(): part = lax.psum_scatter(pair, 'narrow', scatter_dimension=0, tiled=True)]
    all_to_all x2 -> x4, blocking collectives: 125 us -> 109 us  [the longest x1 30.1 us: local(): lax.all_to_all(pieces, 'x', 1, 1).astype(jnp.float32)]
    unnamed x11 -> x12, local copies, waits for them, and re-layouts: 7.08 us -> 8.14 us
  transfers between devices with their start and end apart: 2 -> 1, of which waited for: 2 -> 1; matrix products, arithmetic and copies ran while one was open for 0% -> 0% of each run, Pallas kernels for 0% -> 0%
where the time goes in v3:
time: 246 us; the launch traced here: 245 us
  blocking collectives  170 us (69%)
  waiting for transfers between devices  36.5 us (15%)
  between operations  13.5 us (5%)
  local copies, waits for them, and re-layouts  11.2 us (5%)
  other arithmetic  8.24 us (3%)
  matrix products  6.45 us (3%)
    unnamed x2, waiting for transfers between devices  36.5 us
    all_to_all x1, blocking collectives, local(): lax.all_to_all(pieces, 'x', 1, 1).astype(jnp.float32)  30.1 us
    all_to_all x1, blocking collectives, local(): lax.all_to_all(spread, 'x', 1, 1).reshape(n_z * n_x * rows, tokens.shape[1])  27.7 us
    all_to_all x1, blocking collectives, local(): near = lax.all_to_all(spread, 'z', 0, 0)  27.6 us
    all_to_all x1, blocking collectives, local(): lax.all_to_all(across, 'z', 0, 0).astype(jnp.float32)  23.9 us
    psum x1, blocking collectives, local(): squares = lax.psum(partial, NARROW)  23.7 us
    all_gather x1, blocking collectives, local(): second = lax.all_gather(mine[:, half:], NARROW, axis=0, tiled=True)  18.7 us
    all_gather x1, blocking collectives, local(): first = lax.all_gather(mine[:, :half], NARROW, axis=0, tiled=True)  17.8 us
  transfers between devices with their start and end apart: 1, of which 1 were waited for; matrix products, arithmetic and copies ran while one was open for 0% of the time, Pallas kernels for 0%

profile of v3, /device:TPU:2, one launch (start us, length us, event | category | flops | bytes accessed | tf_op | source)
XLA Modules:
  0.0 245.5 jit_solution(3107269537508157376)
XLA Ops:
  6.5 1.0 broadcast_in_dim.4
  7.6 27.6 %all_to_all.20 = bf16[8,32,1024]{2,1,0:T(8,128)(2,1)S(1)} all-to-all(bf16[8,32,1024]{2,1,0:T(8,128)(2,1)S(1)} %broadcast_in_dim.4), channel_id=1, replica_groups=mesh['z'=8,'x'=4,'y'=8,'core'=2] {'z'}, dimensions={0} | all-to-all | bytes 1048576 | tf_op jit(solution)/shard_map/all_to_all | solution.py:18
  35.2 0.3 broadcast_in_dim.5
  35.4 27.7 %all_to_all.21 = bf16[8,4,32,1024]{3,2,0,1:T(8,128)(2,1)S(1)} all-to-all(bf16[8,4,32,1024]{3,2,0,1:T(8,128)(2,1)S(1)} %broadcast_in_dim.5), channel_id=1, replica_groups=mesh['z'=8,'x'=4,'y'=8,'core'=2] {'x'}, dimensions={1} | all-to-all | bytes 4194304 | tf_op jit(solution)/shard_map/all_to_all | solution.py:20
  63.2 1.3 copy-done.1
  64.5 0.5 multiply_reduce_fusion
  65.0 0.1 reduce_sum.36
  65.1 2.1 copy_convert_fusion
  67.2 0.6 fusion
  67.8 0.0 copy-start.4
  67.8 2.0 convolution_convert_fusion
  69.7 2.0 convolution_convert_fusion.1
  71.7 2.1 pad_maximum_fusion
  73.8 5.6 %copy.17 = bf16[1024,1664]{1,0:T(8,128)(2,1)} copy(bf16[1024,1664]{0,1:T(8,128)(2,1)} %pad_maximum_fusion) | data formatting | bytes 6815744
  79.4 0.0 reduce-scatter.4.cloned.1.call-update
  79.4 23.7 %psum.7 = f32[1024]{0:T(1024)S(1)} all-reduce(f32[1024]{0:T(1024)S(1)} %reduce_sum.36), channel_id=1, replica_groups=mesh['z'=8,'x'=4,'y'=8,'core'=2] {'y','core'}, use_global_device_ids=true, to_apply=%region_2.0 | all-reduce | flops 1024 | bytes 8192 | tf_op jit(solution)/shard_map/psum | solution.py:30
  103.1 0.1 add_rsqrt_fusion
  103.2 36.4 %reduce-scatter.4.cloned.1.call-done = bf16[64,1664]{1,0:T(8,128)(2,1)} async-done(((bf16[1024,1664]{1,0:T(8,128)(2,1)}), bf16[64,1664]{1,0:T(8,128)(2,1)}) %reduce-scatter.4.cloned.1.call-update) | async-done | bytes 213008
  139.7 1.2 copy.18
  140.9 0.1 convert_element_type.30
  140.9 0.1 fusion.5
  141.1 0.7 copy.15
  141.8 0.7 copy.14
  142.5 17.8 %all_gather.6 = bf16[1024,416]{1,0:T(8,128)(2,1)S(1)} all-gather(bf16[64,416]{1,0:T(8,128)(2,1)} %copy.14), channel_id=1, replica_groups=mesh['z'=8,'x'=4,'y'=8,'core'=2] {'y','core'}, dimensions={0}, use_global_device_ids=true | all-gather | bytes 905216 | tf_op jit(solution)/shard_map/all_gather | solution.py:38
  160.4 18.7 %all_gather.7 = bf16[1024,416]{1,0:T(8,128)(2,1)S(1)} all-gather(bf16[64,416]{1,0:T(8,128)(2,1)} %copy.15), channel_id=1, replica_groups=mesh['z'=8,'x'=4,'y'=8,'core'=2] {'y','core'}, dimensions={0}, use_global_device_ids=true | all-gather | bytes 905216 | tf_op jit(solution)/shard_map/all_gather | solution.py:39
  179.1 1.3 fusion.2
  180.3 1.3 add_convert_fusion
  181.6 0.3 copy.16
  181.9 30.1 %all_to_all.22 = bf16[8,4,32,1024]{3,2,0,1:T(8,128)(2,1)} all-to-all(bf16[8,4,32,1024]{3,2,0,1:T(8,128)(2,1)S(1)} %copy.16), channel_id=1, replica_groups=mesh['z'=8,'x'=4,'y'=8,'core'=2] {'x'}, dimensions={1} | all-to-all | bytes 4194304 | tf_op jit(solution)/shard_map/all_to_all | solution.py:43
  212.0 2.0 reduce_sum.37
  214.0 23.9 %all_to_all.23 = bf16[8,32,1024]{2,1,0:T(8,128)(2,1)S(1)} all-to-all(bf16[8,32,1024]{2,1,0:T(8,128)(2,1)S(1)} %reduce_sum.37), channel_id=1, replica_groups=mesh['z'=8,'x'=4,'y'=8,'core'=2] {'z'}, dimensions={0} | all-to-all | bytes 1048576 | tf_op jit(solution)/shard_map/all_to_all | solution.py:44
  237.9 0.7 reduce_sum.38
  (10 shorter events, 0.0 us)
Async XLA Ops:
  6.5 61.2 %copy-start = (bf16[832,1024]{1,0:T(8,128)(2,1)S(1)}, bf16[832,1024]{1,0:T(8,128)(2,1)}, u32[]{:S(2)}) copy-start(bf16[832,1024]{1,0:T(8,128)(2,1)} %param.8) | copy-start | bytes 5111812
  6.5 133.1 %reduce-scatter.4.cloned.1.call-start = ((), (), s32[]{:S(2)}) async-start(), calls=%async_computation.5 | async-start | bytes 3620864
  63.2 1.4 copy-start.1
  65.1 2.1 copy-start.3
  67.8 2.0 copy-start.4
  141.8 37.3 %copy-start.2 = (bf16[832,1024]{1,0:T(8,128)(2,1)S(1)}, bf16[832,1024]{1,0:T(8,128)(2,1)}, u32[]{:S(2)}) copy-start(bf16[832,1024]{1,0:T(8,128)(2,1)} %param.9) | copy-start | bytes 5111812
Sparse Core Ops, SparseCore 0:
  79.5 60.0 reduce-scatter.3

commit v4 on v3

--- a/solution.py
+++ b/solution.py
@@ -22,9 +22,8 @@
     partial = jnp.sum(values * values, axis=1)
     scaled = (values * norm_gain).astype(jnp.bfloat16)
     dims = (((1,), (1,)), ((), ()))
-    gate = lax.dot_general(scaled, gate_weight, dims, preferred_element_type=jnp.float32)
-    upward = lax.dot_general(scaled, up_weight, dims, preferred_element_type=jnp.float32)
-    pair = jnp.concatenate([gate, upward], axis=1).astype(jnp.bfloat16)
+    joined = jnp.concatenate([gate_weight, up_weight], axis=0)
+    pair = lax.dot_general(scaled, joined, dims, preferred_element_type=jnp.float32).astype(jnp.bfloat16)
     pair, partial = lax.optimization_barrier((pair, partial))
     part = lax.psum_scatter(pair, NARROW, scatter_dimension=0, tiled=True)
     squares = lax.psum(partial, NARROW)

time: 246 us -> 234 us (0.951)
  local copies, waits for them, and re-layouts: 11.2 us -> 3.09 us
  other arithmetic: 8.24 us -> 3.87 us
    unnamed x2 -> x1, waiting for transfers between devices: 36.5 us -> 0.02 us
    reduce_scatter x0 -> x1, waiting for transfers between devices: none -> 36.1 us  [local(): part = lax.psum_scatter(pair, NARROW, scatter_dimension=0, tiled=True)]
    unnamed x12 -> x8, local copies, waits for them, and re-layouts: 8.14 us -> 1.58 us
    dot_general x2 -> x1, matrix products: 3.92 us -> 5.39 us  [local(): lax.dot_general(scaled, joined, dims, preferred_element_type=jnp.float32)]
where the time goes in v4:
time: 234 us
  blocking collectives  169 us (72%)
  waiting for transfers between devices  36.1 us (15%)
  between operations  13.5 us (6%)
  matrix products  7.92 us (3%)
  other arithmetic  3.87 us (2%)
  local copies, waits for them, and re-layouts  3.09 us (1%)
    reduce_scatter x1, waiting for transfers between devices, local(): part = lax.psum_scatter(pair, NARROW, scatter_dimension=0, tiled=True)  36.1 us
    all_to_all x1, blocking collectives, local(): lax.all_to_all(pieces, 'x', 1, 1).astype(jnp.float32)  30.2 us
    all_to_all x1, blocking collectives, local(): lax.all_to_all(spread, 'x', 1, 1).reshape(n_z * n_x * rows, tokens.shape[1])  27.7 us
    all_to_all x1, blocking collectives, local(): near = lax.all_to_all(spread, 'z', 0, 0)  27.6 us
    all_to_all x1, blocking collectives, local(): lax.all_to_all(across, 'z', 0, 0).astype(jnp.float32)  23.9 us
    psum x1, blocking collectives, local(): squares = lax.psum(partial, NARROW)  23.8 us
    all_gather x1, blocking collectives, local(): first = lax.all_gather(mine[:, :half], NARROW, axis=0, tiled=True)  18.5 us
    all_gather x1, blocking collectives, local(): second = lax.all_gather(mine[:, half:], NARROW, axis=0, tiled=True)  17.6 us
  transfers between devices with their start and end apart: 1, of which 1 were waited for; matrix products, arithmetic and copies ran while one was open for 0% of the time, Pallas kernels for 0%

profile of v4, /device:TPU:2, one launch (start us, length us, event | category | flops | bytes accessed | tf_op | source)
XLA Modules:
  0.0 233.9 jit_solution(15686111968714107946)
XLA Ops:
  6.5 0.0 reduce-scatter.2.cloned.1.call-start
  6.5 0.9 broadcast_in_dim.4
  7.4 27.6 %all_to_all.20 = bf16[8,32,1024]{2,1,0:T(8,128)(2,1)S(1)} all-to-all(bf16[8,32,1024]{2,1,0:T(8,128)(2,1)S(1)} %broadcast_in_dim.4), channel_id=1, replica_groups=mesh['z'=8,'x'=4,'y'=8,'core'=2] {'z'}, dimensions={0} | all-to-all | bytes 1048576 | tf_op jit(solution)/shard_map/all_to_all | solution.py:18
  35.0 0.3 broadcast_in_dim.5
  35.3 27.7 %all_to_all.21 = bf16[8,4,32,1024]{3,2,0,1:T(8,128)(2,1)S(1)} all-to-all(bf16[8,4,32,1024]{3,2,0,1:T(8,128)(2,1)S(1)} %broadcast_in_dim.5), channel_id=1, replica_groups=mesh['z'=8,'x'=4,'y'=8,'core'=2] {'x'}, dimensions={1} | all-to-all | bytes 4194304 | tf_op jit(solution)/shard_map/all_to_all | solution.py:20
  63.0 0.5 multiply_reduce_fusion
  63.5 0.1 reduce_sum.36
  63.6 0.0 copy-start.1
  63.6 0.5 copy_convert_fusion
  64.1 0.2 copy-done.1
  64.3 0.6 fusion
  64.9 0.8 copy-done.2
  65.7 0.5 copy-done.3
  66.2 5.4 %convolution_convert_fusion = bf16[1024,1664]{1,0:T(8,128)(2,1)} fusion(bf16[1024,1024]{1,0:T(8,128)(2,1)S(1)} %fusion, bf16[832,1024]{1,0:T(8,128)(2,1)S(1)} %copy-done.2, bf16[832,1024]{1,0:T(8,128)(2,1)S(1)} %copy-done.3), kind=kOutput, calls=%fused_computation.4 | convolution fusion | flops 3498180608 | bytes 8912896 | tf_op jit(solution)/shard_map/dot_general | solution.py:26
  71.6 0.0 reduce-scatter.2.cloned.1.call-update
  71.7 0.0 copy-start
  71.7 23.8 %psum.7 = f32[1024]{0:T(1024)S(1)} all-reduce(f32[1024]{0:T(1024)S(1)} %reduce_sum.36), channel_id=1, replica_groups=mesh['z'=8,'x'=4,'y'=8,'core'=2] {'y','core'}, use_global_device_ids=true, to_apply=%region_2.0 | all-reduce | flops 1024 | bytes 8192 | tf_op jit(solution)/shard_map/psum | solution.py:29
  95.5 0.1 add_rsqrt_fusion
  95.6 36.1 %reduce-scatter.2.cloned.1.call-done = bf16[64,1664]{1,0:T(8,128)(2,1)} async-done(((bf16[1024,1664]{1,0:T(8,128)(2,1)}), bf16[64,1664]{1,0:T(8,128)(2,1)}) %reduce-scatter.2.cloned.1.call-update) | async-done | bytes 213008 | tf_op jit(solution)/shard_map/reduce_scatter | solution.py:28
  131.7 1.0 convert_element_type.33
  132.7 0.1 fusion.8
  132.9 0.1 fusion.10
  132.9 17.6 %all_gather.7 = bf16[1024,416]{1,0:T(8,128)(2,1)S(1)} all-gather(bf16[64,416]{1,0:T(8,128)(2,1)S(1)} %get-tuple-element.9), channel_id=1, replica_groups=mesh['z'=8,'x'=4,'y'=8,'core'=2] {'y','core'}, dimensions={0}, use_global_device_ids=true | all-gather | bytes 905216 | tf_op jit(solution)/shard_map/all_gather | solution.py:38
  150.6 18.5 %all_gather.6 = bf16[1024,416]{1,0:T(8,128)(2,1)S(1)} all-gather(bf16[64,416]{1,0:T(8,128)(2,1)S(1)} %get-tuple-element.10), channel_id=1, replica_groups=mesh['z'=8,'x'=4,'y'=8,'core'=2] {'y','core'}, dimensions={0}, use_global_device_ids=true | all-gather | bytes 905216 | tf_op jit(solution)/shard_map/all_gather | solution.py:37
  169.0 0.0 copy-done
  169.0 1.3 fusion.5
  170.3 1.3 add_convert_fusion
  171.6 0.2 copy.10
  171.8 30.2 %all_to_all.22 = bf16[8,4,32,1024]{3,2,0,1:T(8,128)(2,1)S(1)} all-to-all(bf16[8,4,32,1024]{3,2,0,1:T(8,128)(2,1)S(1)} %copy.10), channel_id=1, replica_groups=mesh['z'=8,'x'=4,'y'=8,'core'=2] {'x'}, dimensions={1} | all-to-all | bytes 4194304 | tf_op jit(solution)/shard_map/all_to_all | solution.py:42
  202.0 0.4 reduce_sum.37
  202.4 23.9 %all_to_all.23 = bf16[8,32,1024]{2,1,0:T(8,128)(2,1)S(1)} all-to-all(bf16[8,32,1024]{2,1,0:T(8,128)(2,1)S(1)} %reduce_sum.37), channel_id=1, replica_groups=mesh['z'=8,'x'=4,'y'=8,'core'=2] {'z'}, dimensions={0} | all-to-all | bytes 1048576 | tf_op jit(solution)/shard_map/all_to_all | solution.py:43
  226.3 0.7 reduce_sum.38
  (2 shorter events, 0.0 us)
Async XLA Ops:
  6.5 125.2 %reduce-scatter.2.cloned.1.call-start = ((), (), s32[]{:S(2)}) async-start(), calls=%async_computation.5 | async-start | bytes 3620864 | tf_op jit(solution)/shard_map/reduce_scatter | solution.py:28
  63.6 0.7 copy-start.1
  64.3 1.5 copy-start.2
  64.3 2.0 copy-start.3
  71.7 97.4 %copy-start = (bf16[832,1024]{1,0:T(8,128)(2,1)S(1)}, bf16[832,1024]{1,0:T(8,128)(2,1)}, u32[]{:S(2)}) copy-start(bf16[832,1024]{1,0:T(8,128)(2,1)} %param.9) | copy-start | bytes 5111812
Sparse Core Ops, SparseCore 0:
  71.8 59.9 reduce-scatter.1

commit v5 on v4

--- a/solution.py
+++ b/solution.py
@@ -24,12 +24,15 @@
     dims = (((1,), (1,)), ((), ()))
     joined = jnp.concatenate([gate_weight, up_weight], axis=0)
     pair = lax.dot_general(scaled, joined, dims, preferred_element_type=jnp.float32).astype(jnp.bfloat16)
-    pair, partial = lax.optimization_barrier((pair, partial))
-    part = lax.psum_scatter(pair, NARROW, scatter_dimension=0, tiled=True)
-    squares = lax.psum(partial, NARROW)
-    step = part.shape[0]
-    start = lax.axis_index(NARROW) * step
-    mine_sq = lax.dynamic_slice_in_dim(squares, start, step, 0)
+    n_y = lax.axis_size("y")
+    n_c = lax.axis_size("core")
+    step = pair.shape[0] // (n_y * n_c)
+    pieces = pair.reshape(n_y, n_c, step, pair.shape[1])
+    inner = jnp.sum(lax.all_to_all(pieces, "core", 1, 1).astype(jnp.float32), axis=1).astype(jnp.bfloat16)
+    part = jnp.sum(lax.all_to_all(inner, "y", 0, 0).astype(jnp.float32), axis=0)
+    shares = partial.reshape(n_y, n_c, step)
+    shares = jnp.sum(lax.all_to_all(shares, "core", 1, 1), axis=1)
+    mine_sq = jnp.sum(lax.all_to_all(shares, "y", 0, 0), axis=0)
     scale = lax.rsqrt(mine_sq / model_width + EPS)[:, None]
     sums = part.astype(jnp.float32)
     mine = (jax.nn.silu(sums[:, :width] * scale) * (sums[:, width:] * scale)).astype(jnp.bfloat16)

time: 234 us -> 227 us (0.970)
  blocking collectives: 169 us -> 151 us
  between operations: 13.5 us -> 0.13 us
  waiting for transfers between devices: 36.1 us -> 47.2 us
  starting transfers between devices: 0.01 us -> 10.7 us
  other arithmetic: 3.87 us -> 6.62 us
    all_to_all x0 -> x2, waiting for transfers between devices: none -> 47.2 us  [the longest x1 41.8 us: local(): part = jnp.sum(lax.all_to_all(inner, 'y', 0, 0).astype(jnp.float32), axis=0)]
    reduce_scatter x1 -> x0, waiting for transfers between devices: 36.1 us -> none  [local(): part = lax.psum_scatter(pair, NARROW, scatter_dimension=0, tiled=True)]
    psum x1 -> x0, blocking collectives: 23.8 us -> none  [local(): squares = lax.psum(partial, NARROW)]
    all_to_all x0 -> x2, starting transfers between devices: none -> 10.7 us  [the longest x1 7.1 us: local(): mine_sq = jnp.sum(lax.all_to_all(shares, 'y', 0, 0), axis=0)]
    all_to_all x0 -> x2, blocking collectives: none -> 10.2 us  [the longest x1 6.47 us: local(): lax.all_to_all(pieces, 'core', 1, 1).astype(jnp.float32)]
    all_to_all x1, blocking collectives: 23.9 us -> 19.7 us  [local(): lax.all_to_all(across, 'z', 0, 0).astype(jnp.float32)]
    reduce_sum x0 -> x4, other arithmetic: none -> 3.12 us  [the longest x1 2.27 us: local(): jnp.sum(lax.all_to_all(pieces, 'core', 1, 1).astype(jnp.float32), axis=1)]
  transfers between devices with their start and end apart: 1 -> 2, of which waited for: 1 -> 2; matrix products, arithmetic and copies ran while one was open for 0% -> 1% of each run, Pallas kernels for 0% -> 0%
where the time goes in v5:
time: 227 us; the launch traced here: 226 us
  blocking collectives  151 us (67%)
  waiting for transfers between devices  47.2 us (21%)
  starting transfers between devices  10.7 us (5%)
  matrix products  6.75 us (3%)
  other arithmetic  6.62 us (3%)
  local copies, waits for them, and re-layouts  4.1 us (2%)
    all_to_all x1, waiting for transfers between devices, local(): part = jnp.sum(lax.all_to_all(inner, 'y', 0, 0).astype(jnp.float32), axis=0)  41.8 us
    all_to_all x1, blocking collectives, local(): lax.all_to_all(pieces, 'x', 1, 1).astype(jnp.float32)  29.6 us
    all_to_all x1, blocking collectives, local(): lax.all_to_all(spread, 'x', 1, 1).reshape(n_z * n_x * rows, tokens.shape[1])  27.7 us
    all_to_all x1, blocking collectives, local(): near = lax.all_to_all(spread, 'z', 0, 0)  27.6 us
    all_to_all x1, blocking collectives, local(): lax.all_to_all(across, 'z', 0, 0).astype(jnp.float32)  19.7 us
    all_gather x1, blocking collectives, local(): first = lax.all_gather(mine[:, :half], NARROW, axis=0, tiled=True)  18.6 us
    all_gather x1, blocking collectives, local(): second = lax.all_gather(mine[:, half:], NARROW, axis=0, tiled=True)  17.6 us
    all_to_all x1, starting transfers between devices, local(): mine_sq = jnp.sum(lax.all_to_all(shares, 'y', 0, 0), axis=0)  7.1 us
  transfers between devices with their start and end apart: 2, of which 2 were waited for; matrix products, arithmetic and copies ran while one was open for 1% of the time, Pallas kernels for 0%

profile of v5, /device:TPU:2, one launch (start us, length us, event | category | flops | bytes accessed | tf_op | source)
XLA Modules:
  0.0 226.4 jit_solution(4716993163845403259)
XLA Ops:
  0.0 0.9 broadcast_in_dim.4
  0.9 27.6 %all_to_all.44 = bf16[8,32,1024]{2,1,0:T(8,128)(2,1)S(1)} all-to-all(bf16[8,32,1024]{2,1,0:T(8,128)(2,1)S(1)} %broadcast_in_dim.4), channel_id=1, replica_groups=mesh['z'=8,'x'=4,'y'=8,'core'=2] {'z'}, dimensions={0} | all-to-all | bytes 1048576 | tf_op jit(solution)/shard_map/all_to_all | solution.py:18
  28.5 0.3 broadcast_in_dim.5
  28.8 27.7 %all_to_all.45 = bf16[8,4,32,1024]{3,2,0,1:T(8,128)(2,1)S(1)} all-to-all(bf16[8,4,32,1024]{3,2,0,1:T(8,128)(2,1)S(1)} %broadcast_in_dim.5), channel_id=1, replica_groups=mesh['z'=8,'x'=4,'y'=8,'core'=2] {'x'}, dimensions={1} | all-to-all | bytes 4194304 | tf_op jit(solution)/shard_map/all_to_all | solution.py:20
  56.5 0.5 multiply_reduce_fusion
  57.1 3.7 %all_to_all.46 = f32[2,1,512]{2,1,0:T(1,128)S(1)} all-to-all(f32[2,1,512]{2,1,0:T(1,128)S(1)} %reshape.28), channel_id=1, replica_groups=mesh['z'=8,'x'=4,'y'=8,'core'=2] {'core'}, dimensions={0} | all-to-all | bytes 8192 | tf_op jit(solution)/shard_map/all_to_all | solution.py:34
  60.8 0.5 broadcast.14
  61.3 0.7 reduce.5
  62.1 0.6 bitcast_reduce_fusion
  62.7 0.5 copy_convert_fusion
  63.2 0.2 copy-done.1
  63.4 0.6 fusion
  64.0 0.8 copy-done.2
  64.8 0.5 copy-done.3
  65.3 4.2 %convolution_convert_fusion = bf16[1024,1664]{1,0:T(8,128)(2,1)S(1)} fusion(bf16[1024,1024]{1,0:T(8,128)(2,1)S(1)} %fusion, bf16[832,1024]{1,0:T(8,128)(2,1)S(1)} %copy-done.2, bf16[832,1024]{1,0:T(8,128)(2,1)S(1)} %copy-done.3), kind=kOutput, calls=%fused_computation.4 | convolution fusion | flops 3498180608 | bytes 8912896 | tf_op jit(solution)/shard_map/dot_general | solution.py:26
  69.6 0.3 copy.13
  69.8 6.5 %all_to_all.47 = bf16[8,2,64,1664]{3,2,0,1:T(8,128)(2,1)S(1)} all-to-all(bf16[8,2,64,1664]{3,2,0,1:T(8,128)(2,1)S(1)} %copy.13), channel_id=1, replica_groups=mesh['z'=8,'x'=4,'y'=8,'core'=2] {'core'}, dimensions={1} | all-to-all | bytes 6815744 | tf_op jit(solution)/shard_map/all_to_all | solution.py:31
  76.3 7.1 %all-to-all-start.5 = ((f32[8,1,64]{2,1,0:T(1,128)}), f32[8,1,64]{2,1,0:T(1,128)S(1)}, u32[]{:S(2)}, u32[]{:S(2)}) async-start(f32[8,1,64]{2,1,0:T(1,128)} %bitcast.2), calls=%async_computation.5 | async-start | bytes 8192 | tf_op jit(solution)/shard_map/all_to_all | solution.py:35
  83.4 2.3 %reduce_sum.72 = bf16[8,64,1664]{2,1,0:T(8,128)(2,1)} reduce(bf16[8,2,64,1664]{3,2,0,1:T(8,128)(2,1)S(1)} %all_to_all.47, bf16[]{:T(256)} %constant.9.clone.1), dimensions={1}, to_apply=%region_0.0 | reduce | flops 851968 | bytes 5111810 | tf_op jit(solution)/shard_map/reduce_sum | solution.py:31
  85.7 5.3 %all-to-all-done.5 = f32[8,1,64]{2,1,0:T(1,128)S(1)} async-done(((f32[8,1,64]{2,1,0:T(1,128)}), f32[8,1,64]{2,1,0:T(1,128)S(1)}, u32[]{:S(2)}, u32[]{:S(2)}) %all-to-all-start.5) | async-done | bytes 2080 | tf_op jit(solution)/shard_map/all_to_all | solution.py:35
  91.0 3.6 %all-to-all-start.3 = ((bf16[8,64,1664]{2,1,0:T(8,128)(2,1)}), bf16[8,64,1664]{2,1,0:T(8,128)(2,1)S(1)}, u32[]{:S(2)}, u32[]{:S(2)}) async-start(bf16[8,64,1664]{2,1,0:T(8,128)(2,1)} %reduce_sum.72), calls=%async_computation.3 | async-start | bytes 3407872 | tf_op jit(solution)/shard_map/all_to_all | solution.py:32
  94.7 41.8 %all-to-all-done.3 = bf16[8,64,1664]{2,1,0:T(8,128)(2,1)S(1)} async-done(((bf16[8,64,1664]{2,1,0:T(8,128)(2,1)}), bf16[8,64,1664]{2,1,0:T(8,128)(2,1)S(1)}, u32[]{:S(2)}, u32[]{:S(2)}) %all-to-all-start.3) | async-done | bytes 1703968 | tf_op jit(solution)/shard_map/all_to_all | solution.py:32
  136.5 0.2 convert_reduce_fusion
  137.0 17.6 %all_gather.7 = bf16[1024,416]{1,0:T(8,128)(2,1)S(1)} all-gather(bf16[64,416]{1,0:T(8,128)(2,1)S(1)} %get-tuple-element.5), channel_id=1, replica_groups=mesh['z'=8,'x'=4,'y'=8,'core'=2] {'y','core'}, dimensions={0}, use_global_device_ids=true | all-gather | bytes 905216 | tf_op jit(solution)/shard_map/all_gather | solution.py:41
  154.6 18.6 %all_gather.6 = bf16[1024,416]{1,0:T(8,128)(2,1)S(1)} all-gather(bf16[64,416]{1,0:T(8,128)(2,1)S(1)} %get-tuple-element.6), channel_id=1, replica_groups=mesh['z'=8,'x'=4,'y'=8,'core'=2] {'y','core'}, dimensions={0}, use_global_device_ids=true | all-gather | bytes 905216 | tf_op jit(solution)/shard_map/all_gather | solution.py:40
  173.2 1.3 fusion.5
  174.5 1.3 add_convert_fusion
  175.8 0.3 copy.15
  176.1 29.6 %all_to_all.48 = bf16[8,4,32,1024]{3,2,0,1:T(8,128)(2,1)S(1)} all-to-all(bf16[8,4,32,1024]{3,2,0,1:T(8,128)(2,1)S(1)} %copy.15), channel_id=1, replica_groups=mesh['z'=8,'x'=4,'y'=8,'core'=2] {'x'}, dimensions={1} | all-to-all | bytes 4194304 | tf_op jit(solution)/shard_map/all_to_all | solution.py:45
  205.7 0.4 reduce_sum.77
  206.1 19.7 %all_to_all.49 = bf16[8,32,1024]{2,1,0:T(8,128)(2,1)S(1)} all-to-all(bf16[8,32,1024]{2,1,0:T(8,128)(2,1)S(1)} %reduce_sum.77), channel_id=1, replica_groups=mesh['z'=8,'x'=4,'y'=8,'core'=2] {'z'}, dimensions={0} | all-to-all | bytes 1048576 | tf_op jit(solution)/shard_map/all_to_all | solution.py:46
  225.7 0.7 reduce_sum.78
  (13 shorter events, 0.5 us)
Async XLA Ops:
  62.7 0.7 copy-start.1
  63.4 1.5 copy-start.2
  63.4 2.0 copy-start.3
  76.3 14.7 %all-to-all-start.5 = ((f32[8,1,64]{2,1,0:T(1,128)}), f32[8,1,64]{2,1,0:T(1,128)S(1)}, u32[]{:S(2)}, u32[]{:S(2)}) async-start(f32[8,1,64]{2,1,0:T(1,128)} %bitcast.2), calls=%async_computation.5 | async-start | bytes 8192 | tf_op jit(solution)/shard_map/all_to_all | solution.py:35
  91.0 45.5 %all-to-all-start.3 = ((bf16[8,64,1664]{2,1,0:T(8,128)(2,1)}), bf16[8,64,1664]{2,1,0:T(8,128)(2,1)S(1)}, u32[]{:S(2)}, u32[]{:S(2)}) async-start(bf16[8,64,1664]{2,1,0:T(8,128)(2,1)} %reduce_sum.72), calls=%async_computation.3 | async-start | bytes 3407872 | tf_op jit(solution)/shard_map/all_to_all | solution.py:32
  94.7 78.6 %copy-start = (bf16[832,1024]{1,0:T(8,128)(2,1)S(1)}, bf16[832,1024]{1,0:T(8,128)(2,1)}, u32[]{:S(2)}) copy-start(bf16[832,1024]{1,0:T(8,128)(2,1)} %param.9) | copy-start | bytes 5111812
